TPU v7x, 256 devices: a whole 4x4x8 slice. The times are simulated.
256 devices in a mesh: ctx: 8 (over x, core), ch: 32 (over y, z).
Axes of the slice: x: 4, y: 4, z: 8, core: 2. Of those that a mesh axis runs over, the one named last changes fastest.
Arguments:
- tokens_in: bfloat16 [8192, 8192], P(('ctx', 'ch')), may hold values from -6 to 6
- norm_gain: float32 [8192], replicated, may hold values from 0.1 to 1.9
- proj_weight: bfloat16 [3, 8192, 8192], P(None, 'ctx', 'ch'), may hold values from -0.0625 to 0.0625
- conv_weight: float32 [3, 7, 8192], P(None, None, 'ch'), may hold values from -2 to 2
- decay_rate: float32 [16, 8192], P(None, 'ch'), may hold values from 6.1035157e-06 to 0.04
- residue: float32 [16, 8192], P(None, 'ch'), may hold values from -1.5 to 1.5
- skip_gain: float32 [8192], P('ch'), may hold values from -3 to 3
Outputs:
- gated: bfloat16 [8192, 8192], P(('ctx', 'ch'))
All inputs are finite; a program needn't handle non-finite values.
Results may differ from a plain program's by a relative error of at most 0.008.
Values may be sent and summed in bfloat16 or wider, within the bound.
No kernel may reach another device: no remote copies, remote signals or barrier semaphores. Data moves between devices by JAX's collectives and lax.ppermute only.
A program may use at most 128 MiB of HBM per device.

v0:
```python
import jax
import jax.numpy as jnp
from jax import lax
from jax.sharding import PartitionSpec as P

norm_eps = 1e-05


def shifted(shard, axis, by):
    length = lax.axis_size(axis)
    pairs = [(i, i + by) for i in range(length) if 0 <= i + by < length]
    return lax.ppermute(shard, axis, pairs)


def on_device(tokens_in, norm_gain, proj_weight, conv_weight, decay_rate, residue, skip_gain):
    widened = tokens_in.astype(jnp.float32)
    mean_square = jnp.mean(widened * widened, axis=-1, keepdims=True)
    normed = (widened * lax.rsqrt(mean_square + norm_eps) * norm_gain[None, :]).astype(jnp.bfloat16)
    gathered = lax.all_gather(normed, "ch", axis=0, tiled=True)
    row_count = gathered.shape[0]
    chan_count = proj_weight.shape[2]
    summed = jnp.einsum(
        "tf,ifc->itc",
        gathered,
        lax.all_gather(proj_weight, "ctx", axis=1, tiled=True),
        preferred_element_type=jnp.float32,
    )
    projected = summed.astype(jnp.bfloat16)
    tap_count = conv_weight.shape[1]
    reach = tap_count - 1
    rim_rows = shifted(projected[:, row_count - reach :, :], "ctx", 1)
    padded = jnp.concatenate([rim_rows, projected], axis=1).astype(jnp.float32)
    featured = jnp.zeros((3, row_count, chan_count), jnp.float32)
    for shift_idx in range(tap_count):
        featured = (
            featured
            + conv_weight[:, shift_idx, None, :]
            * padded[:, reach - shift_idx : reach - shift_idx + row_count, :]
        )
    queries = featured[0]
    mixed = featured[1] * featured[2]
    highest = lax.Precision.HIGHEST
    in_scale = jnp.sqrt(-jnp.expm1(-2.0 * decay_rate))
    span_rows = min(128, row_count)
    span_count = row_count // span_rows
    positions = jnp.arange(span_rows, dtype=jnp.float32)
    lag_decay = jnp.exp(-decay_rate[:, None, :] * positions[None, :, None])
    impulse = jnp.sum((residue * in_scale)[:, None, :] * lag_decay, axis=0)
    offsets = jnp.arange(span_rows)[:, None] - jnp.arange(span_rows)[None, :]
    lag_table = (offsets[None, :, :] == jnp.arange(span_rows)[:, None, None]).astype(jnp.float32)
    toeplitz = jnp.einsum("lc,lts->cts", impulse, lag_table, precision=highest)
    spans_in = mixed.reshape(span_count, span_rows, chan_count)
    inside = jnp.einsum("cts,jsc->jtc", toeplitz, spans_in, precision=highest)
    end_weight = in_scale[:, None, :] * jnp.exp(
        -decay_rate[:, None, :] * (span_rows - 1.0 - positions)[None, :, None]
    )
    span_ends = jnp.einsum("jsc,msc->jmc", spans_in, end_weight, precision=highest)
    span_decay = jnp.exp(-decay_rate * float(span_rows))

    def advance(carried, span_end):
        return (span_decay * carried + span_end, carried)

    zero_state = jnp.zeros(decay_rate.shape, jnp.float32)
    local_end, starts = lax.scan(advance, zero_state, span_ends)
    whole_decay = jnp.exp(-decay_rate * float(row_count))

    def handoff(unused_turn, incoming):
        return shifted(whole_decay * incoming + local_end, "ctx", 1)

    incoming = lax.fori_loop(0, lax.axis_size("ctx") - 1, handoff, zero_state)
    span_starts = jnp.arange(span_count, dtype=jnp.float32) * float(span_rows)
    starts = (
        starts
        + jnp.exp(-decay_rate[None, :, :] * span_starts[:, None, None]) * incoming[None, :, :]
    )
    out_weight = residue[:, None, :] * jnp.exp(
        -decay_rate[:, None, :] * (positions + 1.0)[None, :, None]
    )
    outside = jnp.einsum("jmc,mtc->jtc", starts, out_weight, precision=highest)
    filtered = (inside + outside).reshape(row_count, chan_count)
    gated = (queries * (filtered + skip_gain[None, :] * mixed)).astype(jnp.bfloat16)
    return lax.all_to_all(gated, "ch", split_axis=0, concat_axis=1, tiled=True)


def solution(mesh):
    in_specs = (
        P(("ctx", "ch"), None),
        P(),
        P(None, "ctx", "ch"),
        P(None, None, "ch"),
        P(None, "ch"),
        P(None, "ch"),
        P("ch"),
    )
    out_specs = P(("ctx", "ch"), None)
    return jax.shard_map(
        on_device, mesh=mesh, in_specs=in_specs, out_specs=out_specs, check_vma=False
    )
```

profile of v0, /device:TPU:34, one launch (start us, length us, event | category | flops | bytes accessed | tf_op | source)
XLA Modules:
  0.0 376.8 jit_solution(1986812862186608656)
XLA Ops:
  6.5 0.0 copy-start.3
  6.5 0.0 copy-start.1
  6.5 0.0 copy-start.2
  6.5 0.0 all-gather.5.cloned.1.call-start
  6.5 0.7 all-gather.5.cloned.1.call-update
  7.3 0.0 all-gather.3.cloned.1.call-start
  7.3 1.3 fusion.38
  8.6 2.0 fusion.40
  10.6 0.0 all-gather.3.cloned.1.call-update
  10.6 0.0 copy-done.3
  10.6 0.0 copy-done.1
  10.7 0.1 copy.28
  10.8 0.1 copy.27
  10.9 1.7 multiply_reduce_fusion
  12.6 0.0 copy-done.2
  12.7 9.6 %fusion.4 = f32[256,128,128]{2,0,1:T(8,128)} fusion(s32[128,128]{1,0:T(8,128)S(1)} %iota_subtract_fusion, f32[128,256]{0,1:T(8,128)S(1)} %multiply_reduce_fusion), kind=kOutput, calls=%fused_computation.8 | convolution fusion | flops 6444548096 | bytes 16973824 | tf_op jit(solution)/shard_map/lc,lts->cts/dot_general | solution.py:51
  22.2 58.8 %all-gather.5.cloned.1.call-done = bf16[3,8192,256]{2,1,0:T(8,128)(2,1)} async-done(((bf16[3,1024,256]{2,1,0:T(8,128)(2,1)}), bf16[3,8192,256]{2,1,0:T(8,128)(2,1)}) %all-gather.5.cloned.1.call-update) | async-done | bytes 12582928 | tf_op jit(solution)/shard_map/all_gather | solution.py:25
  81.0 141.5 %all-gather.3.cloned.1.call-done = bf16[1024,8192]{1,0:T(8,128)(2,1)} async-done(((bf16[32,8192]{1,0:T(8,128)(2,1)}), bf16[1024,8192]{1,0:T(8,128)(2,1)}) %all-gather.3.cloned.1.call-update) | async-done | bytes 16777232 | tf_op jit(solution)/shard_map/all_gather | solution.py:19
  222.6 18.7 %fusion.23 = bf16[3,1024,256]{2,1,0:T(8,128)(2,1)S(1)} fusion(bf16[3,8192,256]{2,1,0:T(8,128)(2,1)} %all-gather.5.cloned.1.call-done, bf16[1024,8192]{1,0:T(8,128)(2,1)} %all-gather.3.cloned.1.call-done), kind=kOutput, calls=%fused_computation.34 | convolution fusion | flops 12885688320 | bytes 30932992 | tf_op jit(solution)/shard_map/tf,ifc->itc/dot_general | solution.py:22
  241.3 2.1 collective-permute-start.1
  243.4 0.7 copy.31
  244.2 0.1 copy.32
  244.3 2.0 collective-permute-done.1
  246.3 0.3 maximum_convert_fusion
  246.6 2.6 fusion.6
  249.2 0.2 slice_multiply_fusion.7
  249.4 0.4 copy.29
  249.8 38.4 %fusion.32 = f32[8,128,256]{1,0,2:T(8,128)} fusion(f32[8,128,256]{1,0,2:T(8,128)S(1)} %copy.29, f32[256,128,128]{2,0,1:T(8,128)} %fusion.4), kind=kOutput, calls=%fused_computation.37 | convolution fusion | flops 402653184 | bytes 18874368 | tf_op jit(solution)/shard_map/cts,jsc->jtc/dot_general | solution.py:53
  288.2 5.2 %fusion.29 = f32[8,16,256]{1,0,2:T(8,128)} fusion(f32[8,128,256]{1,0,2:T(8,128)S(1)} %copy.29, f32[128]{0:T(128)S(1)} %iota_subtract_fusion.1, f32[16,256]{0,1:T(8,128)S(1)} %copy.32, f32[16,256]{0,1:T(8,128)S(1)} %copy.28), kind=kOutput, calls=%fused_computation.36 | convolution fusion | flops 51380224 | bytes 1212928 | tf_op jit(solution)/shard_map/jsc,msc->jmc/dot_general | solution.py:57
  293.4 0.0 copy-start
  293.4 1.6 copy.34
  295.0 4.9 %while.24 = (s32[]{:T(128)}, f32[16,256]{1,0:T(8,128)S(1)}, f32[8,16,256]{2,1,0:T(8,128)}, f32[16,256]{1,0:T(8,128)S(1)}, f32[8,16,256]{2,1,0:T(8,128)S(1)}, /*index=5*/s32[]{:T(128)}, s32[]{:T(128)}) while((s32[]{:T(128)}, f32[16,256]{1,0:T(8,128)S(1)}, f32[8,16,256]{2,1,0:T(8,128)}, f32[16,256]{1,0:T(8,128)S(1)}, ...), condition=%wide.region_3.4_spmd.clone, body=%wide.region_2.3_spmd.clone.sunk | while | flops 16387 | bytes 98408 | solution.py:64
  295.0 0.6 bitcast_dynamic-update-slice_fusion.2
  295.6 0.6 bitcast_dynamic-update-slice_fusion.2
  296.2 0.6 bitcast_dynamic-update-slice_fusion.2
  296.8 0.6 bitcast_dynamic-update-slice_fusion.2
  297.4 0.6 bitcast_dynamic-update-slice_fusion.2
  298.1 0.6 bitcast_dynamic-update-slice_fusion.2
  298.7 0.6 bitcast_dynamic-update-slice_fusion.2
  299.3 0.6 bitcast_dynamic-update-slice_fusion.2
  299.9 35.4 %while.23 = (s32[]{:T(128)}, f32[16,256]{1,0:T(8,128)S(1)}, f32[16,256]{1,0:T(8,128)S(1)}, f32[16,256]{1,0:T(8,128)S(1)}, s32[]{:T(128)}) while((s32[]{:T(128)}, f32[16,256]{1,0:T(8,128)S(1)}, f32[16,256]{1,0:T(8,128)S(1)}, f32[16,256]{1,0:T(8,128)S(1)}, s32[]{:T(128)}) %tuple.55), condition=%wide.region_5.6_spmd, body=%wide.region_4.5_spmd.sunk | while | flops 8194 | bytes 131173 | solution.py:70
  299.9 1.9 collective-permute-start
  301.9 3.1 collective-permute-done
  305.0 1.9 collective-permute-start
  306.9 3.1 collective-permute-done
  310.1 1.9 collective-permute-start
  312.0 3.1 collective-permute-done
  315.1 1.9 collective-permute-start
  317.0 3.1 collective-permute-done
  320.2 1.9 collective-permute-start
  322.1 3.1 collective-permute-done
  325.2 1.9 collective-permute-start
  327.1 3.1 collective-permute-done
  330.3 1.9 collective-permute-start
  332.2 3.1 collective-permute-done
  335.3 1.0 multiply_add_fusion.1
  336.3 1.3 copy.35
  337.7 0.0 copy-done
  337.7 5.0 %fusion.35 = f32[8,128,256]{1,0,2:T(8,128)} fusion(f32[8,128,256]{1,0,2:T(8,128)S(1)} %copy-done, f32[8,16,256]{1,0,2:T(8,128)} %copy.35, f32[128]{0:T(128)S(1)} %iota_add_fusion, f32[16,256]{0,1:T(8,128)} %copy.31, f32[16,256]{0,1:T(8,128)S(1)} %copy.28), kind=kOutput, calls=%fused_computation.38 | convolution fusion | flops 51642368 | bytes 2261504 | tf_op jit(solution)/shard_map/jmc,mtc->jtc/dot_general | solution.py:79
  342.6 1.6 copy.36
  344.2 0.0 copy-done.4
  344.2 0.4 multiply_convert_fusion
  344.6 24.5 %all_to_all.16 = bf16[32,32,256]{2,1,0:T(8,128)(2,1)S(1)} all-to-all(bf16[32,32,256]{2,1,0:T(8,128)(2,1)S(1)} %multiply_convert_fusion), channel_id=1, replica_groups=mesh['ctx'=8,'ch'=32] {'ch'}, dimensions={0} | all-to-all | bytes 1048576 | tf_op jit(solution)/shard_map/all_to_all | solution.py:82
  369.1 0.8 copy.45
  (31 shorter events, 0.2 us)
Async XLA Ops:
  6.5 4.1 %copy-start.3 = (f32[16,256]{1,0:T(8,128)S(1)}, f32[16,256]{1,0:T(8,128)}, u32[]{:S(2)}) copy-start(f32[16,256]{1,0:T(8,128)} %param.15) | copy-start | bytes 49156
  6.5 4.1 %copy-start.1 = (f32[16,256]{1,0:T(8,128)S(1)}, f32[16,256]{1,0:T(8,128)}, u32[]{:S(2)}) copy-start(f32[16,256]{1,0:T(8,128)} %param.16) | copy-start | bytes 49156
  6.5 6.1 %copy-start.2 = (f32[3,7,256]{2,1,0:T(8,128)S(1)}, f32[3,7,256]{2,1,0:T(8,128)}, u32[]{:S(2)}) copy-start(f32[3,7,256]{2,1,0:T(8,128)} %param.14) | copy-start | bytes 64516
  6.5 74.5 %all-gather.5.cloned.1.call-start = ((), (), s32[]{:S(2)}) async-start(), calls=%async_computation.2 | async-start | bytes 14155776 | tf_op jit(solution)/shard_map/all_gather | solution.py:25
  7.3 215.3 %all-gather.3.cloned.1.call-start = ((), (), s32[]{:S(2)}) async-start(), calls=%async_computation.1 | async-start | bytes 17301504 | tf_op jit(solution)/shard_map/all_gather | solution.py:19
  241.3 5.0 %collective-permute-start.1 = (bf16[3,6,256]{2,1,0:T(8,128)(2,1)S(1)}, bf16[3,6,256]{2,1,0:T(8,128)(2,1)S(1)}, u32[]{:S(2)}, u32[]{:S(2)}) collective-permute-start(bf16[3,6,256]{2,1,0:T(8,128)(2,1)S(1)} %slice.72), channel_id=1, source_target_pairs={{0,32},{32,64},{64,96},{96,128},{128,160},{160,192},{192,224},{1,3... | collective-permute-start | bytes 27656 | tf_op jit(solution)/shard_map/ppermute | solution.py:12
  293.4 44.3 %copy-start = (f32[8,128,256]{1,0,2:T(8,128)S(1)}, f32[8,128,256]{1,0,2:T(8,128)}, u32[]{:S(2)}) copy-start(f32[8,128,256]{1,0,2:T(8,128)} %fusion.32) | copy-start | bytes 3145732
  299.9 5.1 %collective-permute-start = (f32[16,256]{1,0:T(8,128)S(1)}, f32[16,256]{1,0:T(8,128)S(1)}, u32[]{:S(2)}, u32[]{:S(2)}) collective-permute-start(f32[16,256]{1,0:T(8,128)S(1)} %multiply_add_fusion.3), channel_id=1, source_target_pairs={{0,32},{32,64},{64,96},{96,128},{128,160},{160,192},{192,224},{1,3... | collective-permute-start | bytes 49160 | tf_op jit(solution)/shard_map/while/body/eval_jaxpr/ppermute | solution.py:12
  305.0 5.0 %collective-permute-start = (f32[16,256]{1,0:T(8,128)S(1)}, f32[16,256]{1,0:T(8,128)S(1)}, u32[]{:S(2)}, u32[]{:S(2)}) collective-permute-start(f32[16,256]{1,0:T(8,128)S(1)} %multiply_add_fusion.3), channel_id=1, source_target_pairs={{0,32},{32,64},{64,96},{96,128},{128,160},{160,192},{192,224},{1,3... | collective-permute-start | bytes 49160 | tf_op jit(solution)/shard_map/while/body/eval_jaxpr/ppermute | solution.py:12
  310.1 5.0 %collective-permute-start = (f32[16,256]{1,0:T(8,128)S(1)}, f32[16,256]{1,0:T(8,128)S(1)}, u32[]{:S(2)}, u32[]{:S(2)}) collective-permute-start(f32[16,256]{1,0:T(8,128)S(1)} %multiply_add_fusion.3), channel_id=1, source_target_pairs={{0,32},{32,64},{64,96},{96,128},{128,160},{160,192},{192,224},{1,3... | collective-permute-start | bytes 49160 | tf_op jit(solution)/shard_map/while/body/eval_jaxpr/ppermute | solution.py:12
  315.1 5.0 %collective-permute-start = (f32[16,256]{1,0:T(8,128)S(1)}, f32[16,256]{1,0:T(8,128)S(1)}, u32[]{:S(2)}, u32[]{:S(2)}) collective-permute-start(f32[16,256]{1,0:T(8,128)S(1)} %multiply_add_fusion.3), channel_id=1, source_target_pairs={{0,32},{32,64},{64,96},{96,128},{128,160},{160,192},{192,224},{1,3... | collective-permute-start | bytes 49160 | tf_op jit(solution)/shard_map/while/body/eval_jaxpr/ppermute | solution.py:12
  320.2 5.0 %collective-permute-start = (f32[16,256]{1,0:T(8,128)S(1)}, f32[16,256]{1,0:T(8,128)S(1)}, u32[]{:S(2)}, u32[]{:S(2)}) collective-permute-start(f32[16,256]{1,0:T(8,128)S(1)} %multiply_add_fusion.3), channel_id=1, source_target_pairs={{0,32},{32,64},{64,96},{96,128},{128,160},{160,192},{192,224},{1,3... | collective-permute-start | bytes 49160 | tf_op jit(solution)/shard_map/while/body/eval_jaxpr/ppermute | solution.py:12
  325.2 5.0 %collective-permute-start = (f32[16,256]{1,0:T(8,128)S(1)}, f32[16,256]{1,0:T(8,128)S(1)}, u32[]{:S(2)}, u32[]{:S(2)}) collective-permute-start(f32[16,256]{1,0:T(8,128)S(1)} %multiply_add_fusion.3), channel_id=1, source_target_pairs={{0,32},{32,64},{64,96},{96,128},{128,160},{160,192},{192,224},{1,3... | collective-permute-start | bytes 49160 | tf_op jit(solution)/shard_map/while/body/eval_jaxpr/ppermute | solution.py:12
  330.3 5.0 %collective-permute-start = (f32[16,256]{1,0:T(8,128)S(1)}, f32[16,256]{1,0:T(8,128)S(1)}, u32[]{:S(2)}, u32[]{:S(2)}) collective-permute-start(f32[16,256]{1,0:T(8,128)S(1)} %multiply_add_fusion.3), channel_id=1, source_target_pairs={{0,32},{32,64},{64,96},{96,128},{128,160},{160,192},{192,224},{1,3... | collective-permute-start | bytes 49160 | tf_op jit(solution)/shard_map/while/body/eval_jaxpr/ppermute | solution.py:12
  337.7 6.5 %copy-start.4 = (f32[256]{0:T(256)S(1)}, f32[256]{0:T(256)}, u32[]{:S(2)}) copy-start(f32[256]{0:T(256)} %param.17) | copy-start | bytes 3076
Sparse Core Ops, SparseCore 0:
  9.2 71.7 all-gather.4
  83.6 138.9 all-gather.2
where the time goes:
time: 377 us
  waiting for transfers between devices  225 us (60%)
  matrix products  76.7 us (20%)
  blocking collectives  24.5 us (6%)
  starting transfers between devices  15.5 us (4%)
  other arithmetic  14.5 us (4%)
  between operations  13.6 us (4%)
  local copies, waits for them, and re-layouts  6.84 us (2%)
    all_gather x1, waiting for transfers between devices, on_device(): gathered = lax.all_gather(normed, 'ch', axis=0, tiled=True)  142 us
    all_gather x1, waiting for transfers between devices, on_device(): lax.all_gather(proj_weight, 'ctx', axis=1, tiled=True)  58.8 us
    dot_general x1, matrix products, on_device(): inside = jnp.einsum('cts,jsc->jtc', toeplitz, spans_in, precision=highest)  38.4 us
    all_to_all x1, blocking collectives, on_device(): return lax.all_to_all(gated, 'ch', split_axis=0, concat_axis=1, tiled=True)  24.5 us
    ppermute x8, waiting for transfers between devices, shifted(): return lax.ppermute(shard, axis, pairs)  23.9 us
    dot_general x1, matrix products, on_device(): jnp.einsum('tf,ifc->itc', gathered, lax.all_gather(proj_weight, 'ctx', ax...  18.7 us
    ppermute x8, starting transfers between devices, shifted(): return lax.ppermute(shard, axis, pairs)  15.5 us
    dot_general x1, matrix products, on_device(): toeplitz = jnp.einsum('lc,lts->cts', impulse, lag_table, precision=highest)  9.55 us
  transfers between devices with their start and end apart: 10, of which 10 were waited for; matrix products, arithmetic and copies ran while one was open for 4% of the time, Pallas kernels for 0%

commit v1 on v0

--- a/solution.py
+++ b/solution.py
@@ -79,7 +79,9 @@
     outside = jnp.einsum("jmc,mtc->jtc", starts, out_weight, precision=highest)
     filtered = (inside + outside).reshape(row_count, chan_count)
     gated = (queries * (filtered + skip_gain[None, :] * mixed)).astype(jnp.bfloat16)
-    return lax.all_to_all(gated, "ch", split_axis=0, concat_axis=1, tiled=True)
+    return jnp.concatenate(
+        lax.all_to_all(jnp.stack(jnp.split(gated, lax.axis_size("ch"), axis=0)), "ch", 0, 0), axis=1
+    )
 
 
 def solution(mesh):

time: 377 us -> 383 us (1.016)
  no operation moved by 1% of the time
where the time goes in v1:
time: 383 us
  waiting for transfers between devices  225 us (59%)
  matrix products  77.1 us (20%)
  blocking collectives  24.5 us (6%)
  other arithmetic  16.5 us (4%)
  starting transfers between devices  15.5 us (4%)
  between operations  13.8 us (4%)
  local copies, waits for them, and re-layouts  10 us (3%)
    all_gather x1, waiting for transfers between devices, on_device(): gathered = lax.all_gather(normed, 'ch', axis=0, tiled=True)  142 us
    all_gather x1, waiting for transfers between devices, on_device(): lax.all_gather(proj_weight, 'ctx', axis=1, tiled=True)  58.8 us
    dot_general x1, matrix products, on_device(): inside = jnp.einsum('cts,jsc->jtc', toeplitz, spans_in, precision=highest)  38.8 us
    all_to_all x1, blocking collectives, on_device(): lax.all_to_all(jnp.stack(jnp.split(gated, lax.axis_size('ch'), axis=0)),...  24.5 us
    ppermute x8, waiting for transfers between devices, shifted(): return lax.ppermute(shard, axis, pairs)  23.9 us
    dot_general x1, matrix products, on_device(): jnp.einsum('tf,ifc->itc', gathered, lax.all_gather(proj_weight, 'ctx', ax...  18.7 us
    ppermute x8, starting transfers between devices, shifted(): return lax.ppermute(shard, axis, pairs)  15.5 us
    dot_general x1, matrix products, on_device(): toeplitz = jnp.einsum('lc,lts->cts', impulse, lag_table, precision=highest)  9.55 us
  transfers between devices with their start and end apart: 10, of which 10 were waited for; matrix products, arithmetic and copies ran while one was open for 4% of the time, Pallas kernels for 0%

profile of v1, /device:TPU:34, one launch (start us, length us, event | category | flops | bytes accessed | tf_op | source)
XLA Modules:
  0.0 382.5 jit_solution(1816211882507729699)
XLA Ops:
  6.5 0.0 copy-start.3
  6.5 0.0 copy-start.1
  6.5 0.0 copy-start.2
  6.5 0.0 all-gather.5.cloned.1.call-start
  6.5 0.7 all-gather.5.cloned.1.call-update
  7.3 0.0 all-gather.3.cloned.1.call-start
  7.3 1.3 fusion.38
  8.6 2.0 fusion.40
  10.6 0.0 all-gather.3.cloned.1.call-update
  10.6 0.0 copy-done.3
  10.6 0.0 copy-done.1
  10.7 0.1 copy.28
  10.8 0.1 copy.27
  10.9 1.7 multiply_reduce_fusion
  12.6 0.0 copy-done.2
  12.7 9.6 %fusion.4 = f32[256,128,128]{2,0,1:T(8,128)} fusion(s32[128,128]{1,0:T(8,128)S(1)} %iota_subtract_fusion, f32[128,256]{0,1:T(8,128)S(1)} %multiply_reduce_fusion), kind=kOutput, calls=%fused_computation.8 | convolution fusion | flops 6444548096 | bytes 16973824 | tf_op jit(solution)/shard_map/lc,lts->cts/dot_general | solution.py:51
  22.2 58.8 %all-gather.5.cloned.1.call-done = bf16[3,8192,256]{2,1,0:T(8,128)(2,1)} async-done(((bf16[3,1024,256]{2,1,0:T(8,128)(2,1)}), bf16[3,8192,256]{2,1,0:T(8,128)(2,1)}) %all-gather.5.cloned.1.call-update) | async-done | bytes 12582928 | tf_op jit(solution)/shard_map/all_gather | solution.py:25
  81.0 141.5 %all-gather.3.cloned.1.call-done = bf16[1024,8192]{1,0:T(8,128)(2,1)} async-done(((bf16[32,8192]{1,0:T(8,128)(2,1)}), bf16[1024,8192]{1,0:T(8,128)(2,1)}) %all-gather.3.cloned.1.call-update) | async-done | bytes 16777232 | tf_op jit(solution)/shard_map/all_gather | solution.py:19
  222.6 18.7 %fusion.23 = bf16[3,1024,256]{2,1,0:T(8,128)(2,1)S(1)} fusion(bf16[3,8192,256]{2,1,0:T(8,128)(2,1)} %all-gather.5.cloned.1.call-done, bf16[1024,8192]{1,0:T(8,128)(2,1)} %all-gather.3.cloned.1.call-done), kind=kOutput, calls=%fused_computation.34 | convolution fusion | flops 12885688320 | bytes 30932992 | tf_op jit(solution)/shard_map/tf,ifc->itc/dot_general | solution.py:22
  241.3 2.1 collective-permute-start.1
  243.4 0.8 copy.31
  244.2 0.1 copy.32
  244.3 2.0 collective-permute-done.1
  246.3 0.3 maximum_convert_fusion
  246.6 2.6 fusion.6
  249.2 1.1 slice_multiply_fusion.7
  250.3 2.6 copy.29
  252.9 0.0 copy-start
  252.9 38.8 %fusion.32 = f32[8,128,256]{1,0,2:T(8,128)} fusion(f32[8,128,256]{1,0,2:T(8,128)} %copy.29, f32[256,128,128]{2,0,1:T(8,128)} %fusion.4), kind=kOutput, calls=%fused_computation.37 | convolution fusion | flops 402653184 | bytes 18874368 | tf_op jit(solution)/shard_map/cts,jsc->jtc/dot_general | solution.py:53
  291.7 0.0 copy-done
  291.7 5.2 %fusion.29 = f32[8,16,256]{1,0,2:T(8,128)} fusion(f32[8,128,256]{1,0,2:T(8,128)S(1)} %copy-done, f32[128]{0:T(128)S(1)} %iota_subtract_fusion.1, f32[16,256]{0,1:T(8,128)S(1)} %copy.32, f32[16,256]{0,1:T(8,128)S(1)} %copy.28), kind=kOutput, calls=%fused_computation.36 | convolution fusion | flops 51380224 | bytes 1212928 | tf_op jit(solution)/shard_map/jsc,msc->jmc/dot_general | solution.py:57
  296.8 1.5 copy.34
  298.4 4.9 %while.24 = (s32[]{:T(128)}, f32[16,256]{1,0:T(8,128)S(1)}, f32[8,16,256]{2,1,0:T(8,128)}, f32[16,256]{1,0:T(8,128)S(1)}, f32[8,16,256]{2,1,0:T(8,128)S(1)}, /*index=5*/s32[]{:T(128)}, s32[]{:T(128)}) while((s32[]{:T(128)}, f32[16,256]{1,0:T(8,128)S(1)}, f32[8,16,256]{2,1,0:T(8,128)}, f32[16,256]{1,0:T(8,128)S(1)}, ...), condition=%wide.region_3.4_spmd.clone, body=%wide.region_2.3_spmd.clone.sunk | while | flops 16387 | bytes 98408 | solution.py:64
  298.4 0.6 bitcast_dynamic-update-slice_fusion.2
  299.0 0.6 bitcast_dynamic-update-slice_fusion.2
  299.6 0.6 bitcast_dynamic-update-slice_fusion.2
  300.2 0.6 bitcast_dynamic-update-slice_fusion.2
  300.8 0.6 bitcast_dynamic-update-slice_fusion.2
  301.5 0.6 bitcast_dynamic-update-slice_fusion.2
  302.1 0.6 bitcast_dynamic-update-slice_fusion.2
  302.7 0.6 bitcast_dynamic-update-slice_fusion.2
  303.3 35.4 %while.23 = (s32[]{:T(128)}, f32[16,256]{1,0:T(8,128)S(1)}, f32[16,256]{1,0:T(8,128)S(1)}, f32[16,256]{1,0:T(8,128)S(1)}, s32[]{:T(128)}) while((s32[]{:T(128)}, f32[16,256]{1,0:T(8,128)S(1)}, f32[16,256]{1,0:T(8,128)S(1)}, f32[16,256]{1,0:T(8,128)S(1)}, s32[]{:T(128)}) %tuple.54), condition=%wide.region_5.6_spmd, body=%wide.region_4.5_spmd.sunk | while | flops 8194 | bytes 131173 | solution.py:70
  303.3 1.9 collective-permute-start
  305.3 3.1 collective-permute-done
  308.4 1.9 collective-permute-start
  310.3 3.1 collective-permute-done
  313.5 1.9 collective-permute-start
  315.4 3.1 collective-permute-done
  318.5 1.9 collective-permute-start
  320.4 3.1 collective-permute-done
  323.6 1.9 collective-permute-start
  325.5 3.1 collective-permute-done
  328.6 1.9 collective-permute-start
  330.5 3.1 collective-permute-done
  333.7 1.9 collective-permute-start
  335.6 3.1 collective-permute-done
  338.7 1.0 multiply_add_fusion.1
  339.7 1.3 copy.35
  341.0 4.9 %fusion.35 = f32[8,128,256]{1,0,2:T(8,128)} fusion(f32[8,128,256]{1,0,2:T(8,128)} %fusion.32, f32[8,16,256]{1,0,2:T(8,128)} %copy.35, f32[128]{0:T(128)S(1)} %iota_add_fusion, f32[16,256]{0,1:T(8,128)} %copy.31, f32[16,256]{0,1:T(8,128)S(1)} %copy.28), kind=kOutput, calls=%fused_computation.38 | convolution fusion | flops 51642368 | bytes 2261504 | tf_op jit(solution)/shard_map/jmc,mtc->jtc/dot_general | solution.py:79
  345.9 2.5 copy.36
  348.5 0.0 copy-done.4
  348.5 1.5 fusion.42
  350.3 24.5 %all_to_all.5 = bf16[32,32,256]{2,1,0:T(8,128)(2,1)S(1)} all-to-all(bf16[32,32,256]{2,1,0:T(8,128)(2,1)S(1)} %constant_dynamic-update-slice_fusion), channel_id=1, replica_groups=mesh['ctx'=8,'ch'=32] {'ch'}, dimensions={0} | all-to-all | bytes 1048576 | tf_op jit(solution)/shard_map/all_to_all | solution.py:83
  374.9 0.8 copy.45
  (63 shorter events, 0.3 us)
Async XLA Ops:
  6.5 4.1 %copy-start.3 = (f32[16,256]{1,0:T(8,128)S(1)}, f32[16,256]{1,0:T(8,128)}, u32[]{:S(2)}) copy-start(f32[16,256]{1,0:T(8,128)} %param.15) | copy-start | bytes 49156
  6.5 4.1 %copy-start.1 = (f32[16,256]{1,0:T(8,128)S(1)}, f32[16,256]{1,0:T(8,128)}, u32[]{:S(2)}) copy-start(f32[16,256]{1,0:T(8,128)} %param.16) | copy-start | bytes 49156
  6.5 6.1 %copy-start.2 = (f32[3,7,256]{2,1,0:T(8,128)S(1)}, f32[3,7,256]{2,1,0:T(8,128)}, u32[]{:S(2)}) copy-start(f32[3,7,256]{2,1,0:T(8,128)} %param.14) | copy-start | bytes 64516
  6.5 74.5 %all-gather.5.cloned.1.call-start = ((), (), s32[]{:S(2)}) async-start(), calls=%async_computation.2 | async-start | bytes 14155776 | tf_op jit(solution)/shard_map/all_gather | solution.py:25
  7.3 215.3 %all-gather.3.cloned.1.call-start = ((), (), s32[]{:S(2)}) async-start(), calls=%async_computation.1 | async-start | bytes 17301504 | tf_op jit(solution)/shard_map/all_gather | solution.py:19
  241.3 5.0 %collective-permute-start.1 = (bf16[3,6,256]{2,1,0:T(8,128)(2,1)S(1)}, bf16[3,6,256]{2,1,0:T(8,128)(2,1)S(1)}, u32[]{:S(2)}, u32[]{:S(2)}) collective-permute-start(bf16[3,6,256]{2,1,0:T(8,128)(2,1)S(1)} %slice.72), channel_id=1, source_target_pairs={{0,32},{32,64},{64,96},{96,128},{128,160},{160,192},{192,224},{1,3... | collective-permute-start | bytes 27656 | tf_op jit(solution)/shard_map/ppermute | solution.py:12
  252.9 38.8 %copy-start = (f32[8,128,256]{1,0,2:T(8,128)S(1)}, f32[8,128,256]{1,0,2:T(8,128)}, u32[]{:S(2)}) copy-start(f32[8,128,256]{1,0,2:T(8,128)} %copy.29) | copy-start | bytes 3145732
  303.3 5.1 %collective-permute-start = (f32[16,256]{1,0:T(8,128)S(1)}, f32[16,256]{1,0:T(8,128)S(1)}, u32[]{:S(2)}, u32[]{:S(2)}) collective-permute-start(f32[16,256]{1,0:T(8,128)S(1)} %multiply_add_fusion.3), channel_id=1, source_target_pairs={{0,32},{32,64},{64,96},{96,128},{128,160},{160,192},{192,224},{1,3... | collective-permute-start | bytes 49160 | tf_op jit(solution)/shard_map/while/body/eval_jaxpr/ppermute | solution.py:12
  308.4 5.0 %collective-permute-start = (f32[16,256]{1,0:T(8,128)S(1)}, f32[16,256]{1,0:T(8,128)S(1)}, u32[]{:S(2)}, u32[]{:S(2)}) collective-permute-start(f32[16,256]{1,0:T(8,128)S(1)} %multiply_add_fusion.3), channel_id=1, source_target_pairs={{0,32},{32,64},{64,96},{96,128},{128,160},{160,192},{192,224},{1,3... | collective-permute-start | bytes 49160 | tf_op jit(solution)/shard_map/while/body/eval_jaxpr/ppermute | solution.py:12
  313.5 5.0 %collective-permute-start = (f32[16,256]{1,0:T(8,128)S(1)}, f32[16,256]{1,0:T(8,128)S(1)}, u32[]{:S(2)}, u32[]{:S(2)}) collective-permute-start(f32[16,256]{1,0:T(8,128)S(1)} %multiply_add_fusion.3), channel_id=1, source_target_pairs={{0,32},{32,64},{64,96},{96,128},{128,160},{160,192},{192,224},{1,3... | collective-permute-start | bytes 49160 | tf_op jit(solution)/shard_map/while/body/eval_jaxpr/ppermute | solution.py:12
  318.5 5.0 %collective-permute-start = (f32[16,256]{1,0:T(8,128)S(1)}, f32[16,256]{1,0:T(8,128)S(1)}, u32[]{:S(2)}, u32[]{:S(2)}) collective-permute-start(f32[16,256]{1,0:T(8,128)S(1)} %multiply_add_fusion.3), channel_id=1, source_target_pairs={{0,32},{32,64},{64,96},{96,128},{128,160},{160,192},{192,224},{1,3... | collective-permute-start | bytes 49160 | tf_op jit(solution)/shard_map/while/body/eval_jaxpr/ppermute | solution.py:12
  323.6 5.0 %collective-permute-start = (f32[16,256]{1,0:T(8,128)S(1)}, f32[16,256]{1,0:T(8,128)S(1)}, u32[]{:S(2)}, u32[]{:S(2)}) collective-permute-start(f32[16,256]{1,0:T(8,128)S(1)} %multiply_add_fusion.3), channel_id=1, source_target_pairs={{0,32},{32,64},{64,96},{96,128},{128,160},{160,192},{192,224},{1,3... | collective-permute-start | bytes 49160 | tf_op jit(solution)/shard_map/while/body/eval_jaxpr/ppermute | solution.py:12
  328.6 5.0 %collective-permute-start = (f32[16,256]{1,0:T(8,128)S(1)}, f32[16,256]{1,0:T(8,128)S(1)}, u32[]{:S(2)}, u32[]{:S(2)}) collective-permute-start(f32[16,256]{1,0:T(8,128)S(1)} %multiply_add_fusion.3), channel_id=1, source_target_pairs={{0,32},{32,64},{64,96},{96,128},{128,160},{160,192},{192,224},{1,3... | collective-permute-start | bytes 49160 | tf_op jit(solution)/shard_map/while/body/eval_jaxpr/ppermute | solution.py:12
  333.7 5.0 %collective-permute-start = (f32[16,256]{1,0:T(8,128)S(1)}, f32[16,256]{1,0:T(8,128)S(1)}, u32[]{:S(2)}, u32[]{:S(2)}) collective-permute-start(f32[16,256]{1,0:T(8,128)S(1)} %multiply_add_fusion.3), channel_id=1, source_target_pairs={{0,32},{32,64},{64,96},{96,128},{128,160},{160,192},{192,224},{1,3... | collective-permute-start | bytes 49160 | tf_op jit(solution)/shard_map/while/body/eval_jaxpr/ppermute | solution.py:12
  341.0 7.4 %copy-start.4 = (f32[256]{0:T(256)S(1)}, f32[256]{0:T(256)}, u32[]{:S(2)}) copy-start(f32[256]{0:T(256)} %param.17) | copy-start | bytes 3076
Sparse Core Ops, SparseCore 0:
  9.2 71.7 all-gather.4
  83.6 138.9 all-gather.2
